TPU v7x, 32 devices: a whole 2x2x4 slice. The times are simulated.
32 devices in a mesh: space: 4 (over z), dp: 8 (over y, x, core).
Axes of the slice: x: 2, y: 2, z: 4, core: 2. Of those that a mesh axis runs over, the one named last changes fastest.
Arguments:
- features: bfloat16 [8, 12, 128, 320], P('dp', 'space'), may hold values from -6 to 6
- cotangent: bfloat16 [8, 12, 128, 320], P('dp', 'space'), may hold values from -6 to 6
- norm_gain: float32 [320], replicated, may hold values from 0.1 to 1.9
- norm_bias: float32 [320], replicated, may hold values from -0.5 to 0.5
- weight: bfloat16 [2880, 320], P('dp'), may hold values from -0.109375 to 0.109375
- moment_one: float32 [2880, 320], P('dp'), may hold values from -332.55374 to 332.55374
- moment_two: float32 [2880, 320], P('dp'), may hold values from 768 to 6144
- heights: int32 [8], P('dp'), may hold values from 6 to 12, as said below
- widths: int32 [8], P('dp'), may hold values from 64 to 128, as said below
Outputs:
- block_out: bfloat16 [8, 12, 128, 320], P('dp', 'space')
- input_grad: bfloat16 [8, 12, 128, 320], P('dp', 'space')
- weight_grad: float32 [2880, 320], P('dp')
- adam_update: float32 [2880, 320], P('dp')
Inputs may be any that keep to these rules, and one draw needn't show every extreme that they name: Image i occupies canvas rows 0 to heights[i] - 1; some image has all 12 rows. Image i occupies canvas columns 0 to widths[i] - 1; some image has all 128 columns.
All inputs are finite; a program needn't handle non-finite values.
Results may differ from a plain program's by a relative error of at most 0.017.
Values may be sent and summed in bfloat16 or wider, within the bound.
No kernel may reach another device: no remote copies, remote signals or barrier semaphores. Data moves between devices by JAX's collectives and lax.ppermute only.
A program may use at most 64 MiB of HBM per device.

v0:
```python
import jax
import jax.numpy as jnp
from jax import lax
from jax.sharding import PartitionSpec as P

GROUPS = 32


def with_halo(cells, sides, width):
    for axis, dim in sides:
        count = lax.axis_size(axis)
        ends = count - 1
        head = lax.slice_in_dim(cells, 0, width, axis=dim)
        tail = lax.slice_in_dim(cells, cells.shape[dim] - width, cells.shape[dim], axis=dim)
        cells = jnp.concatenate(
            [
                lax.ppermute(tail, axis, [(i, (i + 1) % count) for i in range(ends)]),
                cells,
                lax.ppermute(head, axis, [((i + 1) % count, i) for i in range(ends)]),
            ],
            axis=dim,
        )
    return cells


def space_sum(parts, axis):
    count = lax.axis_size(axis)
    if count & count - 1:
        return lax.psum(parts, axis)
    step = 1
    while step < count:
        pairs = [(i, i ^ step) for i in range(count)]
        parts = tuple((p + q for p, q in zip(parts, lax.ppermute(parts, axis, pairs))))
        step *= 2
    return parts


def group_sum(values, groups):
    height_dev, width_dev, channels = values.shape
    return values.reshape(height_dev, width_dev, groups, channels // groups).sum(axis=(0, 1, 3))


def spread_groups(statistic, channels):
    return jnp.repeat(statistic, channels // statistic.shape[0])


def pad_columns(padded_rows):
    return jnp.pad(padded_rows, ((0, 0), (1, 1), (0, 0)))


def local(
    features, cotangent, norm_gain, norm_bias, weight, moment_one, moment_two, heights, widths
):
    latent = features[0]
    height_dev, width_dev, channels = latent.shape
    row_ids = lax.axis_index("space") * height_dev + jnp.arange(height_dev, dtype=jnp.int32)
    inside = (
        (row_ids < heights[0])[:, None]
        & (jnp.arange(width_dev, dtype=jnp.int32) < widths[0])[None, :]
    ).astype(jnp.float32)[..., None]
    cell_count = (heights[0] * widths[0] * (channels // GROUPS)).astype(jnp.float32)
    gathered = lax.all_gather(weight, "dp", axis=0, tiled=True)
    tap_weights = gathered.reshape(9, channels, channels)
    values = latent.astype(jnp.float32) * inside
    group_total, squares = space_sum(
        (group_sum(values, GROUPS), group_sum(values * values, GROUPS)), "space"
    )
    center = group_total / cell_count
    spread = squares / cell_count - center * center
    inverse = lax.rsqrt(spread + 1e-05)
    normed = (values - spread_groups(center, channels)) * spread_groups(inverse, channels) * inside
    before = normed * norm_gain + norm_bias
    activated = (jax.nn.silu(before) * inside).astype(jnp.bfloat16)
    act_pad = pad_columns(with_halo(activated, (("space", 0),), 1))
    output = jnp.zeros((height_dev * width_dev, channels), jnp.float32)
    for row_off in range(3):
        for col_off in range(3):
            window = act_pad[row_off : row_off + height_dev, col_off : col_off + width_dev].reshape(
                -1, channels
            )
            output = output + jnp.dot(
                window, tap_weights[row_off * 3 + col_off], preferred_element_type=jnp.float32
            )
    block_out = (output.reshape(height_dev, width_dev, channels) * inside).astype(jnp.bfloat16)
    masked = cotangent[0] * inside.astype(jnp.bfloat16)
    cot_pad = pad_columns(with_halo(masked, (("space", 0),), 1))
    flat_cot = masked.reshape(-1, channels)
    upstream = jnp.zeros((height_dev * width_dev, channels), jnp.float32)
    tap_grads = []
    for row_off in range(3):
        for col_off in range(3):
            tap_index = row_off * 3 + col_off
            window = act_pad[row_off : row_off + height_dev, col_off : col_off + width_dev].reshape(
                -1, channels
            )
            tap_grads.append(
                lax.dot_general(
                    window, flat_cot, (((0,), (0,)), ((), ())), preferred_element_type=jnp.float32
                )
            )
            cot_window = cot_pad[
                2 - row_off : 2 - row_off + height_dev, 2 - col_off : 2 - col_off + width_dev
            ].reshape(-1, channels)
            upstream = upstream + lax.dot_general(
                cot_window,
                tap_weights[tap_index],
                (((1,), (1,)), ((), ())),
                preferred_element_type=jnp.float32,
            )
    weight_terms = jnp.stack(tap_grads).reshape(9 * channels, channels)
    gate_sig = jax.nn.sigmoid(before)
    silu_slope = gate_sig * (1.0 + before * (1.0 - gate_sig))
    scaled = upstream.reshape(height_dev, width_dev, channels) * silu_slope * inside * norm_gain
    local_first = group_sum(scaled, GROUPS)
    local_second = group_sum(scaled * normed, GROUPS)
    dp_size = lax.axis_size("dp")
    grad_piece = lax.psum_scatter(
        weight_terms.astype(jnp.bfloat16).reshape(dp_size, -1, channels),
        "dp",
        scatter_dimension=0,
        tiled=False,
    )
    sum_first, sum_second = space_sum((local_first, local_second), "space")
    grad_piece = lax.psum(grad_piece, "space").astype(jnp.float32)
    first = sum_first / cell_count
    second = sum_second / cell_count
    input_grad = (
        spread_groups(inverse, channels)
        * (scaled - spread_groups(first, channels) - normed * spread_groups(second, channels))
        * inside
    ).astype(jnp.bfloat16)
    first_new = 0.9 * moment_one + 0.1 * grad_piece
    second_new = 0.999 * moment_two + 0.001 * grad_piece * grad_piece
    adam_update = first_new / (1.0 - 0.9**10) / (jnp.sqrt(second_new / (1.0 - 0.999**10)) + 1e-08)
    return (block_out[None], input_grad[None], grad_piece, adam_update)


def solution(mesh):
    placed = (
        P("dp", "space", None, None),
        P("dp", "space", None, None),
        P(),
        P(),
        P("dp", None),
        P("dp", None),
        P("dp", None),
        P("dp"),
        P("dp"),
    )
    return jax.shard_map(
        local,
        mesh=mesh,
        in_specs=placed,
        out_specs=(
            P("dp", "space", None, None),
            P("dp", "space", None, None),
            P("dp", None),
            P("dp", None),
        ),
        check_vma=False,
    )
```

profile of v0, /device:TPU:0, one launch (start us, length us, event | category | flops | bytes accessed | tf_op | source)
XLA Modules:
  0.0 191.6 jit_solution(13779045567825138440)
XLA Ops:
  8.6 1.1 multiply_reduce_fusion.1
  10.0 3.1 %collective-permute-start = (f32[32]{0:T(128)S(1)}, f32[32]{0:T(128)S(1)}, u32[]{:S(2)}, u32[]{:S(2)}) collective-permute-start(f32[32]{0:T(128)S(1)} %reduce_sum.51), channel_id=1, source_target_pairs={{0,8},{8,0},{16,24},{24,16},{1,9},{9,1},{17,25},{25,17},{2,10},{10... | collective-permute-start | bytes 392 | tf_op jit(solution)/shard_map/ppermute | solution.py:33
  13.4 1.2 collective-permute-done
  14.6 3.0 %collective-permute-start.1 = (f32[32]{0:T(128)S(1)}, f32[32]{0:T(128)S(1)}, u32[]{:S(2)}, u32[]{:S(2)}) collective-permute-start(f32[32]{0:T(128)S(1)} %add.163), channel_id=1, source_target_pairs={{0,16},{8,24},{16,0},{24,8},{1,17},{9,25},{17,1},{25,9},{2,18},{10... | collective-permute-start | bytes 392 | tf_op jit(solution)/shard_map/ppermute | solution.py:33
  17.6 1.9 collective-permute-start.3
  19.5 2.6 %collective-permute-done.3 = f32[32]{0:T(128)S(1)} collective-permute-done((f32[32]{0:T(128)S(1)}, f32[32]{0:T(128)S(1)}, u32[]{:S(2)}, u32[]{:S(2)}) %collective-permute-start.3) | collective-permute-done | bytes 160 | tf_op jit(solution)/shard_map/ppermute | solution.py:33
  22.5 1.3 multiply_convert_fusion.4
  23.7 3.5 %collective-permute-start.4 = (bf16[1,128,320]{1,2,0:T(8,128)(2,1)S(1)}, bf16[1,128,320]{1,2,0:T(8,128)(2,1)S(1)}, u32[]{:S(2)}, u32[]{:S(2)}) collective-permute-start(bf16[1,128,320]{1,2,0:T(8,128)(2,1)S(1)} %get-tuple-element.30), channel_id=1, source_target_pairs={{0,8},{8,16},{16,24},{1,9},{9,17},{17,25},{2,10},{10,18},{18,26},{... | collective-permute-start | bytes 245768 | tf_op jit(solution)/shard_map/ppermute | solution.py:17
  27.2 1.3 collective-permute-start.5
  28.5 1.0 bitcast_multiply_fusion.2
  29.5 4.1 %collective-permute-done.5 = bf16[1,128,320]{1,2,0:T(8,128)(2,1)S(1)} collective-permute-done((bf16[1,128,320]{1,2,0:T(8,128)(2,1)S(1)}, bf16[1,128,320]{1,2,0:T(8,128)(2,1)S(1)}, u32[]{:S(2)}, u32[]{:S(2)}) %collective-permute-start.5) | collective-permute-done | bytes 81952 | tf_op jit(solution)/shard_map/ppermute | solution.py:19
  34.0 1.0 fusion.29
  35.0 1.0 fusion.15
  36.0 1.1 fusion.27
  37.1 1.0 fusion.25
  38.1 1.2 fusion.23
  39.4 1.1 fusion.21
  40.4 1.0 fusion.19
  41.4 1.1 fusion.13
  42.5 1.1 fusion.17
  43.6 4.2 %copy.68 = bf16[8,360,320]{1,2,0:T(8,128)(2,1)} copy(bf16[8,360,320]{2,1,0:T(8,128)(2,1)} %bitcast.48) | data formatting | bytes 3686400 | tf_op jit(solution)/shard_map/convert_element_type | solution.py:118
  47.8 38.9 %reduce-scatter.2.cloned.1.call-done = bf16[1,360,320]{1,2,0:T(8,128)(2,1)} async-done(((bf16[8,360,320]{1,2,0:T(8,128)(2,1)}), bf16[1,360,320]{1,2,0:T(8,128)(2,1)}) %reduce-scatter.2.cloned.1.call-update) | async-done | bytes 230416 | tf_op jit(solution)/shard_map/reduce_scatter | solution.py:117
  86.8 0.7 all-gather.3.cloned.1.call-update
  87.5 3.4 %collective-permute-start.6 = (bf16[1,128,320]{1,2,0:T(8,128)(2,1)S(1)}, bf16[1,128,320]{1,2,0:T(8,128)(2,1)S(1)}, u32[]{:S(2)}, u32[]{:S(2)}) collective-permute-start(bf16[1,128,320]{1,2,0:T(8,128)(2,1)S(1)} %get-tuple-element.26), channel_id=1, source_target_pairs={{0,8},{8,16},{16,24},{1,9},{9,17},{17,25},{2,10},{10,18},{18,26},{... | collective-permute-start | bytes 245768 | tf_op jit(solution)/shard_map/ppermute | solution.py:17
  90.9 1.3 collective-permute-start.7
  92.8 1.0 copy.49
  93.8 4.8 %collective-permute-done.7 = bf16[1,128,320]{1,2,0:T(8,128)(2,1)S(1)} collective-permute-done((bf16[1,128,320]{1,2,0:T(8,128)(2,1)S(1)}, bf16[1,128,320]{1,2,0:T(8,128)(2,1)S(1)}, u32[]{:S(2)}, u32[]{:S(2)}) %collective-permute-start.7) | collective-permute-done | bytes 81952 | tf_op jit(solution)/shard_map/ppermute | solution.py:19
  98.7 0.6 copy-done.15
  100.0 0.9 copy.56
  100.9 1.7 pad_maximum_fusion
  102.6 1.8 copy.57
  104.4 0.9 copy.58
  105.3 0.9 copy.59
  106.3 0.9 copy.61
  107.2 0.9 copy.62
  108.1 0.9 copy.63
  109.0 0.9 copy.64
  109.9 1.0 fusion.102
  110.9 1.2 copy.43
  112.1 0.9 copy.45
  113.0 0.9 copy.46
  113.9 0.9 copy.47
  114.8 0.9 copy.51
  115.7 0.9 copy.50
  117.1 7.1 %all-reduce.4.cloned.1.call-done = bf16[360,320]{0,1:T(8,128)(2,1)} async-done(((bf16[360,320]{0,1:T(8,128)(2,1)}), bf16[360,320]{0,1:T(8,128)(2,1)}) %all-reduce.4.cloned.1.call-update) | async-done | bytes 230416 | tf_op jit(solution)/shard_map/psum | solution.py:124
  124.2 2.3 %fusion.35 = (f32[360,320]{0,1:T(8,128)}, f32[360,320]{0,1:T(8,128)}) fusion(f32[360,320]{0,1:T(8,128)S(1)} %copy-done.11, f32[360,320]{0,1:T(8,128)} %param.14, bf16[360,320]{0,1:T(8,128)(2,1)} %all-reduce.4.cloned.1.call-done), kind=kLoop, calls=%fused_computation.65 | loop fusion | flops 1382400 | bytes 2073600 | tf_op jit(solution)/shard_map/div | solution.py:134
  126.5 27.0 %all-gather.3.cloned.1.call-done = bf16[8,360,320]{1,2,0:T(8,128)(2,1)} async-done(((bf16[1,360,320]{1,2,0:T(8,128)(2,1)}), bf16[8,360,320]{1,2,0:T(8,128)(2,1)}) %all-gather.3.cloned.1.call-update) | async-done | bytes 1843216 | tf_op jit(solution)/shard_map/all_gather | solution.py:62
  153.5 4.0 %copy.44 = bf16[8,360,320]{1,0,2:T(8,128)(2,1)} copy(bf16[8,360,320]{1,2,0:T(8,128)(2,1)} %all-gather.3.cloned.1.call-done) | data formatting | bytes 3686400 | tf_op jit(solution)/shard_map/all_gather | solution.py:62
  157.4 3.4 %reshape.284 = bf16[2880,320]{0,1:T(8,128)(2,1)S(1)} reshape(bf16[8,360,320]{1,0,2:T(8,128)(2,1)} %copy.44) | data formatting | bytes 3686400
  161.2 1.3 fusion.68
  164.3 0.5 fusion.2
  166.1 1.4 fusion.81
  167.5 1.5 convolution_add_fusion.8
  169.4 0.5 convolution_add_fusion.6
  170.4 0.5 convolution_add_fusion.4
  171.3 0.5 convolution_add_fusion.2
  172.0 0.7 fusion.100
  173.0 1.6 collective-permute-start.8
  174.7 0.6 collective-permute-start.10
  175.6 1.0 collective-permute-done.8
  176.6 2.4 %collective-permute-start.9 = (f32[32]{0:T(128)S(1)}, f32[32]{0:T(128)S(1)}, u32[]{:S(2)}, u32[]{:S(2)}) collective-permute-start(f32[32]{0:T(128)S(1)} %add.198), channel_id=1, source_target_pairs={{0,16},{8,24},{16,0},{24,8},{1,17},{9,25},{17,1},{25,9},{2,18},{10... | collective-permute-start | bytes 392 | tf_op jit(solution)/shard_map/ppermute | solution.py:33
  179.0 1.8 collective-permute-start.11
  181.0 2.4 %collective-permute-done.11 = f32[32]{0:T(128)S(1)} collective-permute-done((f32[32]{0:T(128)S(1)}, f32[32]{0:T(128)S(1)}, u32[]{:S(2)}, u32[]{:S(2)}) %collective-permute-start.11) | collective-permute-done | bytes 160 | tf_op jit(solution)/shard_map/ppermute | solution.py:33
  183.8 1.3 multiply_convert_fusion.1
  (100 shorter events, 9.2 us)
Async XLA Ops:
  7.2 79.6 %reduce-scatter.2.cloned.1.call-start = ((), (), s32[]{:S(2)}) async-start(), calls=%async_computation.1 | async-start | bytes 2211840 | tf_op jit(solution)/shard_map/reduce_scatter | solution.py:117
  10.0 4.6 %collective-permute-start = (f32[32]{0:T(128)S(1)}, f32[32]{0:T(128)S(1)}, u32[]{:S(2)}, u32[]{:S(2)}) collective-permute-start(f32[32]{0:T(128)S(1)} %reduce_sum.51), channel_id=1, source_target_pairs={{0,8},{8,0},{16,24},{24,16},{1,9},{9,1},{17,25},{25,17},{2,10},{10... | collective-permute-start | bytes 392 | tf_op jit(solution)/shard_map/ppermute | solution.py:33
  13.3 4.3 %collective-permute-start.2 = (f32[32]{0:T(128)S(1)}, f32[32]{0:T(128)S(1)}, u32[]{:S(2)}, u32[]{:S(2)}) collective-permute-start(f32[32]{0:T(128)S(1)} %reduce_sum.54), channel_id=1, source_target_pairs={{0,8},{8,0},{16,24},{24,16},{1,9},{9,1},{17,25},{25,17},{2,10},{10... | collective-permute-start | bytes 392 | tf_op jit(solution)/shard_map/ppermute | solution.py:33
  14.6 4.9 %collective-permute-start.1 = (f32[32]{0:T(128)S(1)}, f32[32]{0:T(128)S(1)}, u32[]{:S(2)}, u32[]{:S(2)}) collective-permute-start(f32[32]{0:T(128)S(1)} %add.163), channel_id=1, source_target_pairs={{0,16},{8,24},{16,0},{24,8},{1,17},{9,25},{17,1},{25,9},{2,18},{10... | collective-permute-start | bytes 392 | tf_op jit(solution)/shard_map/ppermute | solution.py:33
  17.6 4.4 %collective-permute-start.3 = (f32[32]{0:T(128)S(1)}, f32[32]{0:T(128)S(1)}, u32[]{:S(2)}, u32[]{:S(2)}) collective-permute-start(f32[32]{0:T(128)S(1)} %add.165), channel_id=1, source_target_pairs={{0,16},{8,24},{16,0},{24,8},{1,17},{9,25},{17,1},{25,9},{2,18},{10... | collective-permute-start | bytes 392 | tf_op jit(solution)/shard_map/ppermute | solution.py:33
  23.7 5.8 %collective-permute-start.4 = (bf16[1,128,320]{1,2,0:T(8,128)(2,1)S(1)}, bf16[1,128,320]{1,2,0:T(8,128)(2,1)S(1)}, u32[]{:S(2)}, u32[]{:S(2)}) collective-permute-start(bf16[1,128,320]{1,2,0:T(8,128)(2,1)S(1)} %get-tuple-element.30), channel_id=1, source_target_pairs={{0,8},{8,16},{16,24},{1,9},{9,17},{17,25},{2,10},{10,18},{18,26},{... | collective-permute-start | bytes 245768 | tf_op jit(solution)/shard_map/ppermute | solution.py:17
  27.2 6.3 %collective-permute-start.5 = (bf16[1,128,320]{1,2,0:T(8,128)(2,1)S(1)}, bf16[1,128,320]{1,2,0:T(8,128)(2,1)S(1)}, u32[]{:S(2)}, u32[]{:S(2)}) collective-permute-start(bf16[1,128,320]{1,2,0:T(8,128)(2,1)S(1)} %get-tuple-element.31), channel_id=1, source_target_pairs={{8,0},{16,8},{24,16},{9,1},{17,9},{25,17},{10,2},{18,10},{26,18},{... | collective-permute-start | bytes 245768 | tf_op jit(solution)/shard_map/ppermute | solution.py:19
  34.0 4.2 %copy-start = (bf16[1,3,128,320]{2,3,1,0:T(8,128)(2,1)S(1)}, bf16[1,3,128,320]{2,3,1,0:T(8,128)(2,1)}, u32[]{:S(2)}) copy-start(bf16[1,3,128,320]{2,3,1,0:T(8,128)(2,1)} %param.9) | copy-start | bytes 737284
  34.0 4.2 %copy-start.10 = (bf16[1,3,128,320]{2,3,1,0:T(8,128)(2,1)S(1)}, bf16[1,3,128,320]{2,3,1,0:T(8,128)(2,1)}, u32[]{:S(2)}) copy-start(bf16[1,3,128,320]{2,3,1,0:T(8,128)(2,1)} %param.10) | copy-start | bytes 737284
  34.0 4.1 %copy-start.17 = (f32[320]{0:T(512)S(1)}, f32[320]{0:T(512)}, u32[]{:S(2)}) copy-start(f32[320]{0:T(512)} %param.12) | copy-start | bytes 3844
  34.0 4.1 %copy-start.18 = (f32[320]{0:T(512)S(1)}, f32[320]{0:T(512)}, u32[]{:S(2)}) copy-start(f32[320]{0:T(512)} %param.11) | copy-start | bytes 3844
  47.8 76.4 %all-reduce.4.cloned.1.call-start = ((), (), s32[]{:S(2)}) async-start(), calls=%async_computation.2 | async-start | bytes 491520 | tf_op jit(solution)/shard_map/psum | solution.py:124
  86.8 66.7 %all-gather.3.cloned.1.call-start = ((), (), s32[]{:S(2)}) async-start(), calls=%async_computation.3 | async-start | bytes 2211840 | tf_op jit(solution)/shard_map/all_gather | solution.py:62
  87.5 6.3 %collective-permute-start.6 = (bf16[1,128,320]{1,2,0:T(8,128)(2,1)S(1)}, bf16[1,128,320]{1,2,0:T(8,128)(2,1)S(1)}, u32[]{:S(2)}, u32[]{:S(2)}) collective-permute-start(bf16[1,128,320]{1,2,0:T(8,128)(2,1)S(1)} %get-tuple-element.26), channel_id=1, source_target_pairs={{0,8},{8,16},{16,24},{1,9},{9,17},{17,25},{2,10},{10,18},{18,26},{... | collective-permute-start | bytes 245768 | tf_op jit(solution)/shard_map/ppermute | solution.py:17
  90.9 7.7 %collective-permute-start.7 = (bf16[1,128,320]{1,2,0:T(8,128)(2,1)S(1)}, bf16[1,128,320]{1,2,0:T(8,128)(2,1)S(1)}, u32[]{:S(2)}, u32[]{:S(2)}) collective-permute-start(bf16[1,128,320]{1,2,0:T(8,128)(2,1)S(1)} %get-tuple-element.27), channel_id=1, source_target_pairs={{8,0},{16,8},{24,16},{9,1},{17,9},{25,17},{10,2},{18,10},{26,18},{... | collective-permute-start | bytes 245768 | tf_op jit(solution)/shard_map/ppermute | solution.py:19
  93.8 4.8 %copy-start.14 = (bf16[1,128,320]{1,2,0:T(8,128)(2,1)}, bf16[1,128,320]{1,2,0:T(8,128)(2,1)S(1)}, u32[]{:S(2)}) copy-start(bf16[1,128,320]{1,2,0:T(8,128)(2,1)S(1)} %collective-permute-done.6) | copy-start | bytes 245764
  98.7 0.6 copy-start.15
  113.0 11.2 %copy-start.11 = (f32[360,320]{0,1:T(8,128)S(1)}, f32[360,320]{0,1:T(8,128)}, u32[]{:S(2)}) copy-start(f32[360,320]{0,1:T(8,128)} %param.15) | copy-start | bytes 1382404
  160.8 1.7 copy-start.9
  160.8 2.1 %copy-start.8 = (bf16[3,128,320]{2,1,0:T(8,128)(2,1)S(1)}, bf16[3,128,320]{2,1,0:T(8,128)(2,1)}, u32[]{:S(2)}) copy-start(bf16[3,128,320]{2,1,0:T(8,128)(2,1)} %copy.45) | copy-start | bytes 737284
  161.2 2.1 %copy-start.7 = (bf16[3,128,320]{2,1,0:T(8,128)(2,1)S(1)}, bf16[3,128,320]{2,1,0:T(8,128)(2,1)}, u32[]{:S(2)}) copy-start(bf16[3,128,320]{2,1,0:T(8,128)(2,1)} %copy.46) | copy-start | bytes 737284
  162.5 1.1 copy-start.6
  163.3 1.1 copy-start.12
  166.1 2.9 %copy-start.5 = (bf16[3,128,320]{2,1,0:T(8,128)(2,1)S(1)}, bf16[3,128,320]{2,1,0:T(8,128)(2,1)}, u32[]{:S(2)}) copy-start(bf16[3,128,320]{2,1,0:T(8,128)(2,1)} %copy.58) | copy-start | bytes 737284
  166.1 3.3 %copy-start.4 = (bf16[3,128,320]{2,1,0:T(8,128)(2,1)S(1)}, bf16[3,128,320]{2,1,0:T(8,128)(2,1)}, u32[]{:S(2)}) copy-start(bf16[3,128,320]{2,1,0:T(8,128)(2,1)} %copy.59) | copy-start | bytes 737284
  169.4 1.0 copy-start.3
  169.9 1.0 copy-start.1
  170.3 1.0 copy-start.2
  170.9 1.1 copy-start.13
  170.9 1.1 copy-start.16
  173.0 3.6 %collective-permute-start.8 = (f32[32]{0:T(128)S(1)}, f32[32]{0:T(128)S(1)}, u32[]{:S(2)}, u32[]{:S(2)}) collective-permute-start(f32[32]{0:T(128)S(1)} %reduce_sum.72), channel_id=1, source_target_pairs={{0,8},{8,0},{16,24},{24,16},{1,9},{9,1},{17,25},{25,17},{2,10},{10... | collective-permute-start | bytes 392 | tf_op jit(solution)/shard_map/ppermute | solution.py:33
  174.7 4.3 %collective-permute-start.10 = (f32[32]{0:T(128)S(1)}, f32[32]{0:T(128)S(1)}, u32[]{:S(2)}, u32[]{:S(2)}) collective-permute-start(f32[32]{0:T(128)S(1)} %reduce_sum.75), channel_id=1, source_target_pairs={{0,8},{8,0},{16,24},{24,16},{1,9},{9,1},{17,25},{25,17},{2,10},{10... | collective-permute-start | bytes 392 | tf_op jit(solution)/shard_map/ppermute | solution.py:33
  176.6 4.4 %collective-permute-start.9 = (f32[32]{0:T(128)S(1)}, f32[32]{0:T(128)S(1)}, u32[]{:S(2)}, u32[]{:S(2)}) collective-permute-start(f32[32]{0:T(128)S(1)} %add.198), channel_id=1, source_target_pairs={{0,16},{8,24},{16,0},{24,8},{1,17},{9,25},{17,1},{25,9},{2,18},{10... | collective-permute-start | bytes 392 | tf_op jit(solution)/shard_map/ppermute | solution.py:33
  179.0 4.4 %collective-permute-start.11 = (f32[32]{0:T(128)S(1)}, f32[32]{0:T(128)S(1)}, u32[]{:S(2)}, u32[]{:S(2)}) collective-permute-start(f32[32]{0:T(128)S(1)} %add.200), channel_id=1, source_target_pairs={{0,16},{8,24},{16,0},{24,8},{1,17},{9,25},{17,1},{25,9},{2,18},{10... | collective-permute-start | bytes 392 | tf_op jit(solution)/shard_map/ppermute | solution.py:33
Sparse Core Ops, SparseCore 0:
  47.9 38.8 reduce-scatter.1
  89.2 34.9 all-reduce.3
  126.1 27.3 all-gather.2
where the time goes:
time: 192 us
  waiting for transfers between devices  89.9 us (47%)
  local copies, waits for them, and re-layouts  31.8 us (17%)
  starting transfers between devices  24 us (12%)
  matrix products  20.2 us (11%)
  between operations  15.6 us (8%)
  other arithmetic  10.2 us (5%)
    reduce_scatter x1, waiting for transfers between devices, local(): lax.psum_scatter(weight_terms.astype(jnp.bfloat16).reshape(dp_size, -1, c...  38.9 us
    all_gather x1, waiting for transfers between devices, local(): gathered = lax.all_gather(weight, 'dp', axis=0, tiled=True)  27 us
    ppermute x8, starting transfers between devices, space_sum(): lax.ppermute(parts, axis, pairs)  14.4 us
    dot_general x9, matrix products, local(): lax.dot_general(window, flat_cot, (((0,), (0,)), ((), ())), preferred_ele...  9.52 us
    ppermute x2, waiting for transfers between devices, with_halo(): lax.ppermute(head, axis, [((i + 1) % count, i) for i in range(ends)])  8.87 us
    slice x9, local copies, waits for them, and re-layouts, local(): cot_pad[2 - row_off:2 - row_off + height_dev, 2 - col_off:2 - col_off + w...  8.5 us
    ppermute x8, waiting for transfers between devices, space_sum(): lax.ppermute(parts, axis, pairs)  7.28 us
    slice x9, local copies, waits for them, and re-layouts, local(): act_pad[row_off:row_off + height_dev, col_off:col_off + width_dev]  7.13 us
  transfers between devices with their start and end apart: 15, of which 9 were waited for; matrix products, arithmetic and copies ran while one was open for 12% of the time, Pallas kernels for 0%

commit v1 on v0

--- a/solution.py
+++ b/solution.py
@@ -59,7 +59,13 @@
         & (jnp.arange(width_dev, dtype=jnp.int32) < widths[0])[None, :]
     ).astype(jnp.float32)[..., None]
     cell_count = (heights[0] * widths[0] * (channels // GROUPS)).astype(jnp.float32)
-    gathered = lax.all_gather(weight, "dp", axis=0, tiled=True)
+    peers = lax.axis_size("dp")
+    held, blocks = (weight, [weight])
+    for _ in range(peers - 1):
+        held = lax.ppermute(held, "dp", [(i_2, (i_2 + 1) % peers) for i_2 in range(peers)])
+        blocks.insert(0, held)
+    line = jnp.concatenate(blocks, axis=0)
+    gathered = jnp.roll(line, (lax.axis_index("dp") + 1) * weight.shape[0], axis=0)
     tap_weights = gathered.reshape(9, channels, channels)
     values = latent.astype(jnp.float32) * inside
     group_total, squares = space_sum(

time: 192 us -> 181 us (0.943)
  waiting for transfers between devices: 89.9 us -> 73.8 us
  matrix products: 20.2 us -> 30.3 us
  local copies, waits for them, and re-layouts: 31.8 us -> 27.8 us
  starting transfers between devices: 24 us -> 21.9 us
    reduce_scatter x1, waiting for transfers between devices: 38.9 us -> 0.02 us  [local(): lax.psum_scatter(weight_terms.astype(jnp.bfloat16).reshape(dp_size, -1, c...]
    ppermute x0 -> x7, waiting for transfers between devices: none -> 31.4 us  [local(): lax.ppermute(held, 'dp', [(i_2, (i_2 + 1) % peers) for i_2 in range(peers)])]
    all_gather x1 -> x0, waiting for transfers between devices: 27 us -> none  [local(): gathered = lax.all_gather(weight, 'dp', axis=0, tiled=True)]
    psum x1, waiting for transfers between devices: 7.13 us -> 32.7 us  [local(): grad_piece = lax.psum(grad_piece, 'space').astype(jnp.float32)]
    ppermute x2, waiting for transfers between devices: 8.87 us -> 0.01 us  [with_halo(): lax.ppermute(head, axis, [((i + 1) % count, i) for i in range(ends)])]
    dot_general x9, matrix products: 4.33 us -> 12.6 us  [local(): jnp.dot(window, tap_weights[row_off * 3 + col_off], preferred_element_typ...]
    dot_general x9, matrix products: 6.32 us -> 14.4 us  [local(): lax.dot_general(cot_window, tap_weights[tap_index], (((1,), (1,)), ((), (...]
    concatenate x0 -> x1, local copies, waits for them, and re-layouts: none -> 7.64 us  [local(): jnp.roll(line, (lax.axis_index('dp') + 1) * weight.shape[0], axis=0)]
  transfers between devices with their start and end apart: 15 -> 21, of which waited for: 9 -> 13; matrix products, arithmetic and copies ran while one was open for 12% -> 35% of each run, Pallas kernels for 0% -> 0%
where the time goes in v1:
time: 181 us; the launch traced here: 179 us
  waiting for transfers between devices  73.8 us (41%)
  matrix products  30.3 us (17%)
  local copies, waits for them, and re-layouts  27.8 us (15%)
  starting transfers between devices  21.9 us (12%)
  between operations  16.3 us (9%)
  other arithmetic  8.81 us (5%)
    psum x1, waiting for transfers between devices, local(): grad_piece = lax.psum(grad_piece, 'space').astype(jnp.float32)  32.7 us
    ppermute x7, waiting for transfers between devices, local(): lax.ppermute(held, 'dp', [(i_2, (i_2 + 1) % peers) for i_2 in range(peers)])  31.4 us
    dot_general x9, matrix products, local(): lax.dot_general(cot_window, tap_weights[tap_index], (((1,), (1,)), ((), (...  14.4 us
    dot_general x9, matrix products, local(): jnp.dot(window, tap_weights[row_off * 3 + col_off], preferred_element_typ...  12.6 us
    ppermute x8, starting transfers between devices, space_sum(): lax.ppermute(parts, axis, pairs)  11.6 us
    ppermute x8, waiting for transfers between devices, space_sum(): lax.ppermute(parts, axis, pairs)  9.65 us
    concatenate x1, local copies, waits for them, and re-layouts, local(): jnp.roll(line, (lax.axis_index('dp') + 1) * weight.shape[0], axis=0)  7.64 us
    slice x9, local copies, waits for them, and re-layouts, local(): cot_pad[2 - row_off:2 - row_off + height_dev, 2 - col_off:2 - col_off + w...  7.52 us
  transfers between devices with their start and end apart: 21, of which 13 were waited for; matrix products, arithmetic and copies ran while one was open for 35% of the time, Pallas kernels for 0%

profile of v1, /device:TPU:0, one launch (start us, length us, event | category | flops | bytes accessed | tf_op | source)
XLA Modules:
  0.0 178.9 jit_solution(14504432050021784574)
XLA Ops:
  8.7 1.1 multiply_reduce_fusion.1
  10.1 3.1 %collective-permute-start = (f32[32]{0:T(128)S(1)}, f32[32]{0:T(128)S(1)}, u32[]{:S(2)}, u32[]{:S(2)}) collective-permute-start(f32[32]{0:T(128)S(1)} %reduce_sum.51), channel_id=1, source_target_pairs={{0,8},{8,0},{16,24},{24,16},{1,9},{9,1},{17,25},{25,17},{2,10},{10... | collective-permute-start | bytes 392 | tf_op jit(solution)/shard_map/ppermute | solution.py:33
  13.5 1.0 bitcast_multiply_fusion.2
  14.5 3.9 %collective-permute-start.13 = (bf16[1,128,320]{1,2,0:T(8,128)(2,1)S(1)}, bf16[1,128,320]{1,2,0:T(8,128)(2,1)S(1)}, u32[]{:S(2)}, u32[]{:S(2)}) collective-permute-start(bf16[1,128,320]{1,2,0:T(8,128)(2,1)S(1)} %get-tuple-element.26), channel_id=1, source_target_pairs={{0,8},{8,16},{16,24},{1,9},{9,17},{17,25},{2,10},{10,18},{18,26},{... | collective-permute-start | bytes 245768 | tf_op jit(solution)/shard_map/ppermute | solution.py:17
  18.4 1.3 collective-permute-start.14
  19.7 0.7 fusion.123
  20.4 1.1 copy.21
  21.5 1.2 copy.33
  22.7 0.8 bitcast_multiply_fusion.1
  23.5 3.7 %collective-permute-start.1 = (f32[32]{0:T(128)S(1)}, f32[32]{0:T(128)S(1)}, u32[]{:S(2)}, u32[]{:S(2)}) collective-permute-start(f32[32]{0:T(128)S(1)} %add.176), channel_id=1, source_target_pairs={{0,16},{8,24},{16,0},{24,8},{1,17},{9,25},{17,1},{25,9},{2,18},{10... | collective-permute-start | bytes 392 | tf_op jit(solution)/shard_map/ppermute | solution.py:33
  27.5 1.2 collective-permute-done.1
  28.7 2.9 %collective-permute-done.3 = f32[32]{0:T(128)S(1)} collective-permute-done((f32[32]{0:T(128)S(1)}, f32[32]{0:T(128)S(1)}, u32[]{:S(2)}, u32[]{:S(2)}) %collective-permute-start.3) | collective-permute-done | bytes 160 | tf_op jit(solution)/shard_map/ppermute | solution.py:33
  32.4 3.5 %collective-permute-start.4 = (bf16[1,128,320]{1,2,0:T(8,128)(2,1)S(1)}, bf16[1,128,320]{1,2,0:T(8,128)(2,1)S(1)}, u32[]{:S(2)}, u32[]{:S(2)}) collective-permute-start(bf16[1,128,320]{1,2,0:T(8,128)(2,1)S(1)} %get-tuple-element.30), channel_id=1, source_target_pairs={{0,8},{8,16},{16,24},{1,9},{9,17},{17,25},{2,10},{10,18},{18,26},{... | collective-permute-start | bytes 245768 | tf_op jit(solution)/shard_map/ppermute | solution.py:17
  35.9 1.3 collective-permute-start.5
  37.9 0.9 copy.32
  38.8 0.9 copy.31
  39.7 0.9 copy.34
  40.6 0.9 copy.35
  41.5 0.9 copy.37
  42.4 0.9 copy.30
  43.3 0.9 copy.36
  44.2 0.9 copy.29
  45.2 0.7 copy-done.24
  46.6 1.4 fusion.138
  49.1 6.4 %collective-permute-done.7 = bf16[360,320]{0,1:T(8,128)(2,1)S(1)} collective-permute-done((bf16[360,320]{0,1:T(8,128)(2,1)}, bf16[360,320]{0,1:T(8,128)(2,1)S(1)}, u32[]{:S(2)}, u32[]{:S(2)}) %collective-permute-start.7) | collective-permute-done | bytes 230432 | tf_op jit(solution)/shard_map/ppermute | solution.py:65
  55.5 0.5 fusion.35
  56.0 6.0 %collective-permute-done.8 = bf16[360,320]{0,1:T(8,128)(2,1)S(1)} collective-permute-done((bf16[360,320]{0,1:T(8,128)(2,1)S(1)}, bf16[360,320]{0,1:T(8,128)(2,1)S(1)}, u32[]{:S(2)}, u32[]{:S(2)}) %collective-permute-start.8) | collective-permute-done | bytes 230432 | tf_op jit(solution)/shard_map/ppermute | solution.py:65
  62.4 6.1 %collective-permute-done.9 = bf16[360,320]{0,1:T(8,128)(2,1)S(1)} collective-permute-done((bf16[360,320]{0,1:T(8,128)(2,1)S(1)}, bf16[360,320]{0,1:T(8,128)(2,1)S(1)}, u32[]{:S(2)}, u32[]{:S(2)}) %collective-permute-start.9) | collective-permute-done | bytes 230432 | tf_op jit(solution)/shard_map/ppermute | solution.py:65
  68.9 6.2 %collective-permute-done.10 = bf16[360,320]{0,1:T(8,128)(2,1)S(1)} collective-permute-done((bf16[360,320]{0,1:T(8,128)(2,1)S(1)}, bf16[360,320]{0,1:T(8,128)(2,1)S(1)}, u32[]{:S(2)}, u32[]{:S(2)}) %collective-permute-start.10) | collective-permute-done | bytes 230432 | tf_op jit(solution)/shard_map/ppermute | solution.py:65
  75.4 6.3 %collective-permute-done.11 = bf16[360,320]{0,1:T(8,128)(2,1)} collective-permute-done((bf16[360,320]{0,1:T(8,128)(2,1)S(1)}, bf16[360,320]{0,1:T(8,128)(2,1)}, u32[]{:S(2)}, u32[]{:S(2)}) %collective-permute-start.11) | collective-permute-done | bytes 230432 | tf_op jit(solution)/shard_map/ppermute | solution.py:65
  81.7 0.4 fusion.29
  82.1 2.6 %copy.41 = bf16[8,360,320]{1,2,0:T(8,128)(2,1)} copy(bf16[8,360,320]{2,1,0:T(8,128)(2,1)S(1)} %bitcast.202) | data formatting | bytes 3686400 | tf_op jit(solution)/shard_map/convert_element_type | solution.py:124
  85.0 1.3 copy.26
  88.0 0.5 collective-permute-done.12
  88.5 7.6 %concatenate.25 = bf16[5760,320]{0,1:T(8,128)(2,1)} concatenate(bf16[360,320]{0,1:T(8,128)(2,1)} %collective-permute-done.12, bf16[360,320]{0,1:T(8,128)(2,1)} %collective-permute-done.11, bf16[360,320]{0,1:T(8,128)(2,1)} %copy-done.19, bf16[360,320]{0,1:T(8,128)(2,1)} %copy-done.18, bf16[360,320]{0,1:T(8,128)(2,1)} %copy-done.17, bf16[360,320]{0,1:T(8,128)(2,1)} %copy-done.16, ...), dimensions={0} | concatenate | bytes 7372800 | tf_op jit(solution)/shard_map/jit(_roll_dynamic)/concatenate | solution.py:68
  96.2 1.4 fusion.72
  97.6 1.4 fusion.80
  98.9 1.4 fusion.84
  100.3 1.4 fusion.91
  101.7 1.4 fusion.95
  103.0 1.4 fusion.76
  104.4 1.4 fusion.99
  105.8 1.6 fusion.69
  107.4 1.4 fusion.14
  109.3 0.5 copy-done.7
  109.8 1.5 fusion.89
  111.3 1.6 fusion.93
  112.9 1.6 fusion.82
  114.5 1.6 fusion.78
  116.1 1.6 fusion.70
  117.7 1.5 fusion.97
  119.2 1.6 fusion.74
  120.8 1.5 fusion.86
  122.4 2.0 %fusion.136 = (f32[320]{0:T(512)S(1)}, f32[320]{0:T(512)S(1)}, f32[384,320]{0,1:T(8,128)S(1)}) fusion(f32[320]{0:T(512)S(1)} %mul.299, f32[320]{0:T(512)S(1)} %sub.59, f32[384,320]{0,1:T(8,128)S(1)} %copy.22, f32[384]{0:T(512)S(1)} %copy-done.30, f32[320]{0:T(512)S(1)} %copy-done.27, f32[320]{0:T(512)S(1)} %copy-done.29, f32[384,320]{0,1:T(8,128)S(1)} %fusion.70, ...), kind=kOutput, calls=%fused_computation.183 | convolution fusion | flops 81960320 | bytes 5415940 | tf_op jit(solution)/shard_map/dot_general | solution.py:110
  124.6 2.6 %collective-permute-start.15 = (f32[32]{0:T(128)S(1)}, f32[32]{0:T(128)S(1)}, u32[]{:S(2)}, u32[]{:S(2)}) collective-permute-start(f32[32]{0:T(128)S(1)} %reduce_sum.72), channel_id=1, source_target_pairs={{0,8},{8,0},{16,24},{24,16},{1,9},{9,1},{17,25},{25,17},{2,10},{10... | collective-permute-start | bytes 392 | tf_op jit(solution)/shard_map/ppermute | solution.py:33
  127.7 1.0 collective-permute-done.15
  128.7 1.4 collective-permute-start.16
  130.1 0.9 collective-permute-done.17
  131.0 0.6 collective-permute-start.18
  131.9 1.3 collective-permute-done.16
  133.2 2.3 %collective-permute-done.18 = f32[32]{0:T(128)S(1)} collective-permute-done((f32[32]{0:T(128)S(1)}, f32[32]{0:T(128)S(1)}, u32[]{:S(2)}, u32[]{:S(2)}) %collective-permute-start.18) | collective-permute-done | bytes 160 | tf_op jit(solution)/shard_map/ppermute | solution.py:33
  135.9 1.3 multiply_convert_fusion.1
  137.2 32.7 %all-reduce.4.cloned.1.call-done = bf16[360,320]{0,1:T(8,128)(2,1)} async-done(((bf16[360,320]{0,1:T(8,128)(2,1)}), bf16[360,320]{0,1:T(8,128)(2,1)}) %all-reduce.4.cloned.1.call-update) | async-done | bytes 230416 | tf_op jit(solution)/shard_map/psum | solution.py:130
  169.8 2.2 %fusion.47 = (f32[360,320]{0,1:T(8,128)}, f32[360,320]{0,1:T(8,128)}) fusion(f32[360,320]{0,1:T(8,128)S(1)} %copy-done.20, f32[360,320]{0,1:T(8,128)S(1)} %copy-done.21, bf16[360,320]{0,1:T(8,128)(2,1)} %all-reduce.4.cloned.1.call-done), kind=kLoop, calls=%fused_computation.65 | loop fusion | flops 1382400 | bytes 2073600 | tf_op jit(solution)/shard_map/div | solution.py:140
  (140 shorter events, 9.1 us)
Async XLA Ops:
  7.2 24.8 %copy-start = (bf16[1,3,128,320]{2,3,1,0:T(8,128)(2,1)S(1)}, bf16[1,3,128,320]{2,3,1,0:T(8,128)(2,1)}, u32[]{:S(2)}) copy-start(bf16[1,3,128,320]{2,3,1,0:T(8,128)(2,1)} %param.9) | copy-start | bytes 737284
  7.2 24.8 %copy-start.28 = (f32[320]{0:T(512)S(1)}, f32[320]{0:T(512)}, u32[]{:S(2)}) copy-start(f32[320]{0:T(512)} %param.11) | copy-start | bytes 3844
  7.2 24.8 %copy-start.27 = (f32[320]{0:T(512)S(1)}, f32[320]{0:T(512)}, u32[]{:S(2)}) copy-start(f32[320]{0:T(512)} %param.12) | copy-start | bytes 3844
  7.2 128.7 %reduce-scatter.2.cloned.1.call-start = ((), (), s32[]{:S(2)}) async-start(), calls=%async_computation.1 | async-start | bytes 2211840 | tf_op jit(solution)/shard_map/reduce_scatter | solution.py:123
  8.7 22.9 %copy-start.31 = (bf16[3,128]{1,0:T(4,128)(2,1)}, bf16[3,128]{1,0:T(4,128)(2,1)S(1)}, u32[]{:S(2)}) copy-start(bf16[3,128]{1,0:T(4,128)(2,1)S(1)} %get-tuple-element.37) | copy-start | bytes 2308
  10.1 13.4 %collective-permute-start = (f32[32]{0:T(128)S(1)}, f32[32]{0:T(128)S(1)}, u32[]{:S(2)}, u32[]{:S(2)}) collective-permute-start(f32[32]{0:T(128)S(1)} %reduce_sum.51), channel_id=1, source_target_pairs={{0,8},{8,0},{16,24},{24,16},{1,9},{9,1},{17,25},{25,17},{2,10},{10... | collective-permute-start | bytes 392 | tf_op jit(solution)/shard_map/ppermute | solution.py:33
  13.4 13.8 %collective-permute-start.2 = (f32[32]{0:T(128)S(1)}, f32[32]{0:T(128)S(1)}, u32[]{:S(2)}, u32[]{:S(2)}) collective-permute-start(f32[32]{0:T(128)S(1)} %reduce_sum.54), channel_id=1, source_target_pairs={{0,8},{8,0},{16,24},{24,16},{1,9},{9,1},{17,25},{25,17},{2,10},{10... | collective-permute-start | bytes 392 | tf_op jit(solution)/shard_map/ppermute | solution.py:33
  13.5 35.2 %collective-permute-start.6 = (bf16[360,320]{0,1:T(8,128)(2,1)}, bf16[360,320]{0,1:T(8,128)(2,1)}, u32[]{:S(2)}, u32[]{:S(2)}) collective-permute-start(bf16[360,320]{0,1:T(8,128)(2,1)} %param.13), channel_id=1, source_target_pairs={{0,1},{1,2},{2,3},{3,4},{4,5},{5,6},{6,7},{7,0},{8,9},{9,10},{10,1... | collective-permute-start | bytes 691208 | tf_op jit(solution)/shard_map/ppermute | solution.py:65
  14.5 22.6 %collective-permute-start.13 = (bf16[1,128,320]{1,2,0:T(8,128)(2,1)S(1)}, bf16[1,128,320]{1,2,0:T(8,128)(2,1)S(1)}, u32[]{:S(2)}, u32[]{:S(2)}) collective-permute-start(bf16[1,128,320]{1,2,0:T(8,128)(2,1)S(1)} %get-tuple-element.26), channel_id=1, source_target_pairs={{0,8},{8,16},{16,24},{1,9},{9,17},{17,25},{2,10},{10,18},{18,26},{... | collective-permute-start | bytes 245768 | tf_op jit(solution)/shard_map/ppermute | solution.py:17
  18.4 18.8 %collective-permute-start.14 = (bf16[1,128,320]{1,2,0:T(8,128)(2,1)S(1)}, bf16[1,128,320]{1,2,0:T(8,128)(2,1)S(1)}, u32[]{:S(2)}, u32[]{:S(2)}) collective-permute-start(bf16[1,128,320]{1,2,0:T(8,128)(2,1)S(1)} %get-tuple-element.27), channel_id=1, source_target_pairs={{8,0},{16,8},{24,16},{9,1},{17,9},{25,17},{10,2},{18,10},{26,18},{... | collective-permute-start | bytes 245768 | tf_op jit(solution)/shard_map/ppermute | solution.py:19
  23.5 5.2 %collective-permute-start.1 = (f32[32]{0:T(128)S(1)}, f32[32]{0:T(128)S(1)}, u32[]{:S(2)}, u32[]{:S(2)}) collective-permute-start(f32[32]{0:T(128)S(1)} %add.176), channel_id=1, source_target_pairs={{0,16},{8,24},{16,0},{24,8},{1,17},{9,25},{17,1},{25,9},{2,18},{10... | collective-permute-start | bytes 392 | tf_op jit(solution)/shard_map/ppermute | solution.py:33
  27.2 4.4 %collective-permute-start.3 = (f32[32]{0:T(128)S(1)}, f32[32]{0:T(128)S(1)}, u32[]{:S(2)}, u32[]{:S(2)}) collective-permute-start(f32[32]{0:T(128)S(1)} %add.178), channel_id=1, source_target_pairs={{0,16},{8,24},{16,0},{24,8},{1,17},{9,25},{17,1},{25,9},{2,18},{10... | collective-permute-start | bytes 392 | tf_op jit(solution)/shard_map/ppermute | solution.py:33
  32.4 12.8 %collective-permute-start.4 = (bf16[1,128,320]{1,2,0:T(8,128)(2,1)S(1)}, bf16[1,128,320]{1,2,0:T(8,128)(2,1)S(1)}, u32[]{:S(2)}, u32[]{:S(2)}) collective-permute-start(bf16[1,128,320]{1,2,0:T(8,128)(2,1)S(1)} %get-tuple-element.30), channel_id=1, source_target_pairs={{0,8},{8,16},{16,24},{1,9},{9,17},{17,25},{2,10},{10,18},{18,26},{... | collective-permute-start | bytes 245768 | tf_op jit(solution)/shard_map/ppermute | solution.py:17
  35.9 9.3 %collective-permute-start.5 = (bf16[1,128,320]{1,2,0:T(8,128)(2,1)S(1)}, bf16[1,128,320]{1,2,0:T(8,128)(2,1)S(1)}, u32[]{:S(2)}, u32[]{:S(2)}) collective-permute-start(bf16[1,128,320]{1,2,0:T(8,128)(2,1)S(1)} %get-tuple-element.31), channel_id=1, source_target_pairs={{8,0},{16,8},{24,16},{9,1},{17,9},{25,17},{10,2},{18,10},{26,18},{... | collective-permute-start | bytes 245768 | tf_op jit(solution)/shard_map/ppermute | solution.py:19
  45.1 2.8 %copy-start.22 = (bf16[1,128,320]{1,2,0:T(8,128)(2,1)}, bf16[1,128,320]{1,2,0:T(8,128)(2,1)S(1)}, u32[]{:S(2)}) copy-start(bf16[1,128,320]{1,2,0:T(8,128)(2,1)S(1)} %collective-permute-done.4) | copy-start | bytes 245764
  45.2 0.7 copy-start.24
  46.5 9.0 %copy-start.10 = (bf16[1,3,128,320]{2,3,1,0:T(8,128)(2,1)S(1)}, bf16[1,3,128,320]{2,3,1,0:T(8,128)(2,1)}, u32[]{:S(2)}) copy-start(bf16[1,3,128,320]{2,3,1,0:T(8,128)(2,1)} %param.10) | copy-start | bytes 737284
  46.5 9.0 %copy-start.32 = (bf16[3,128]{1,0:T(4,128)(2,1)S(1)}, bf16[3,128]{1,0:T(4,128)(2,1)}, u32[]{:S(2)}) copy-start(bf16[3,128]{1,0:T(4,128)(2,1)} %copy-done.31) | copy-start | bytes 2308
  48.7 6.8 %collective-permute-start.7 = (bf16[360,320]{0,1:T(8,128)(2,1)}, bf16[360,320]{0,1:T(8,128)(2,1)S(1)}, u32[]{:S(2)}, u32[]{:S(2)}) collective-permute-start(bf16[360,320]{0,1:T(8,128)(2,1)} %collective-permute-done.6), channel_id=1, source_target_pairs={{0,1},{1,2},{2,3},{3,4},{4,5},{5,6},{6,7},{7,0},{8,9},{9,10},{10,1... | collective-permute-start | bytes 691208 | tf_op jit(solution)/shard_map/ppermute | solution.py:65
  49.1 26.0 %copy-start.25 = (bf16[1,128,320]{1,2,0:T(8,128)(2,1)S(1)}, bf16[1,128,320]{1,2,0:T(8,128)(2,1)}, u32[]{:S(2)}) copy-start(bf16[1,128,320]{1,2,0:T(8,128)(2,1)} %copy-done.24) | copy-start | bytes 245764
  55.5 6.9 %copy-start.16 = (bf16[360,320]{0,1:T(8,128)(2,1)}, bf16[360,320]{0,1:T(8,128)(2,1)S(1)}, u32[]{:S(2)}) copy-start(bf16[360,320]{0,1:T(8,128)(2,1)S(1)} %collective-permute-done.7) | copy-start | bytes 691204
  55.5 6.5 %collective-permute-start.8 = (bf16[360,320]{0,1:T(8,128)(2,1)S(1)}, bf16[360,320]{0,1:T(8,128)(2,1)S(1)}, u32[]{:S(2)}, u32[]{:S(2)}) collective-permute-start(bf16[360,320]{0,1:T(8,128)(2,1)S(1)} %collective-permute-done.7), channel_id=1, source_target_pairs={{0,1},{1,2},{2,3},{3,4},{4,5},{5,6},{6,7},{7,0},{8,9},{9,10},{10,1... | collective-permute-start | bytes 691208 | tf_op jit(solution)/shard_map/ppermute | solution.py:65
  62.0 20.1 %copy-start.17 = (bf16[360,320]{0,1:T(8,128)(2,1)}, bf16[360,320]{0,1:T(8,128)(2,1)S(1)}, u32[]{:S(2)}) copy-start(bf16[360,320]{0,1:T(8,128)(2,1)S(1)} %collective-permute-done.8) | copy-start | bytes 691204
  62.0 6.5 %collective-permute-start.9 = (bf16[360,320]{0,1:T(8,128)(2,1)S(1)}, bf16[360,320]{0,1:T(8,128)(2,1)S(1)}, u32[]{:S(2)}, u32[]{:S(2)}) collective-permute-start(bf16[360,320]{0,1:T(8,128)(2,1)S(1)} %collective-permute-done.8), channel_id=1, source_target_pairs={{0,1},{1,2},{2,3},{3,4},{4,5},{5,6},{6,7},{7,0},{8,9},{9,10},{10,1... | collective-permute-start | bytes 691208 | tf_op jit(solution)/shard_map/ppermute | solution.py:65
  68.5 13.6 %copy-start.18 = (bf16[360,320]{0,1:T(8,128)(2,1)}, bf16[360,320]{0,1:T(8,128)(2,1)S(1)}, u32[]{:S(2)}) copy-start(bf16[360,320]{0,1:T(8,128)(2,1)S(1)} %collective-permute-done.9) | copy-start | bytes 691204
  68.5 6.5 %collective-permute-start.10 = (bf16[360,320]{0,1:T(8,128)(2,1)S(1)}, bf16[360,320]{0,1:T(8,128)(2,1)S(1)}, u32[]{:S(2)}, u32[]{:S(2)}) collective-permute-start(bf16[360,320]{0,1:T(8,128)(2,1)S(1)} %collective-permute-done.9), channel_id=1, source_target_pairs={{0,1},{1,2},{2,3},{3,4},{4,5},{5,6},{6,7},{7,0},{8,9},{9,10},{10,1... | collective-permute-start | bytes 691208 | tf_op jit(solution)/shard_map/ppermute | solution.py:65
  75.1 7.0 %copy-start.19 = (bf16[360,320]{0,1:T(8,128)(2,1)}, bf16[360,320]{0,1:T(8,128)(2,1)S(1)}, u32[]{:S(2)}) copy-start(bf16[360,320]{0,1:T(8,128)(2,1)S(1)} %collective-permute-done.10) | copy-start | bytes 691204
  75.1 6.6 %collective-permute-start.11 = (bf16[360,320]{0,1:T(8,128)(2,1)S(1)}, bf16[360,320]{0,1:T(8,128)(2,1)}, u32[]{:S(2)}, u32[]{:S(2)}) collective-permute-start(bf16[360,320]{0,1:T(8,128)(2,1)S(1)} %collective-permute-done.10), channel_id=1, source_target_pairs={{0,1},{1,2},{2,3},{3,4},{4,5},{5,6},{6,7},{7,0},{8,9},{9,10},{10,1... | collective-permute-start | bytes 691208 | tf_op jit(solution)/shard_map/ppermute | solution.py:65
  81.7 6.8 %collective-permute-start.12 = (bf16[360,320]{0,1:T(8,128)(2,1)}, bf16[360,320]{0,1:T(8,128)(2,1)}, u32[]{:S(2)}, u32[]{:S(2)}) collective-permute-start(bf16[360,320]{0,1:T(8,128)(2,1)} %collective-permute-done.11), channel_id=1, source_target_pairs={{0,1},{1,2},{2,3},{3,4},{4,5},{5,6},{6,7},{7,0},{8,9},{9,10},{10,1... | collective-permute-start | bytes 691208 | tf_op jit(solution)/shard_map/ppermute | solution.py:65
  84.7 1.6 copy-start.15
  84.7 1.9 %copy-start.14 = (bf16[3,128,320]{1,2,0:T(8,128)(2,1)S(1)}, bf16[3,128,320]{1,2,0:T(8,128)(2,1)}, u32[]{:S(2)}) copy-start(bf16[3,128,320]{1,2,0:T(8,128)(2,1)} %get-tuple-element.20) | copy-start | bytes 737284
  84.7 2.1 %copy-start.13 = (bf16[3,128,320]{1,2,0:T(8,128)(2,1)S(1)}, bf16[3,128,320]{1,2,0:T(8,128)(2,1)}, u32[]{:S(2)}) copy-start(bf16[3,128,320]{1,2,0:T(8,128)(2,1)} %get-tuple-element.21) | copy-start | bytes 737284
  84.7 2.3 %copy-start.12 = (bf16[3,128,320]{1,2,0:T(8,128)(2,1)S(1)}, bf16[3,128,320]{1,2,0:T(8,128)(2,1)}, u32[]{:S(2)}) copy-start(bf16[3,128,320]{1,2,0:T(8,128)(2,1)} %get-tuple-element.22) | copy-start | bytes 737284
  84.7 2.6 %copy-start.23 = (bf16[1,128,320]{1,2,0:T(8,128)(2,1)S(1)}, bf16[1,128,320]{1,2,0:T(8,128)(2,1)}, u32[]{:S(2)}) copy-start(bf16[1,128,320]{1,2,0:T(8,128)(2,1)} %copy-done.22) | copy-start | bytes 245764
  84.7 2.6 %copy-start.26 = (bf16[1,128,320]{1,2,0:T(8,128)(2,1)S(1)}, bf16[1,128,320]{1,2,0:T(8,128)(2,1)}, u32[]{:S(2)}) copy-start(bf16[1,128,320]{1,2,0:T(8,128)(2,1)} %copy-done.24) | copy-start | bytes 245764
  84.8 85.1 %all-reduce.4.cloned.1.call-start = ((), (), s32[]{:S(2)}) async-start(), calls=%async_computation.2 | async-start | bytes 491520 | tf_op jit(solution)/shard_map/psum | solution.py:130
  86.3 1.4 copy-start.11
  100.3 5.5 %copy-start.29 = (f32[320]{0:T(512)S(1)}, f32[320]{0:T(512)}, u32[]{:S(2)}) copy-start(f32[320]{0:T(512)} %param.11) | copy-start | bytes 3844
  100.3 5.5 %copy-start.33 = (f32[384]{0:T(512)S(1)}, f32[384]{0:T(512)}, u32[]{:S(2)}) copy-start(f32[384]{0:T(512)} %get-tuple-element.36) | copy-start | bytes 4612
  108.9 1.0 copy-start.7
  108.9 2.5 %copy-start.6 = (bf16[3,128,320]{2,1,0:T(8,128)(2,1)S(1)}, bf16[3,128,320]{2,1,0:T(8,128)(2,1)}, u32[]{:S(2)}) copy-start(bf16[3,128,320]{2,1,0:T(8,128)(2,1)} %copy.31) | copy-start | bytes 737284
  108.9 4.1 %copy-start.5 = (bf16[3,128,320]{2,1,0:T(8,128)(2,1)S(1)}, bf16[3,128,320]{2,1,0:T(8,128)(2,1)}, u32[]{:S(2)}) copy-start(bf16[3,128,320]{2,1,0:T(8,128)(2,1)} %copy.34) | copy-start | bytes 737284
  109.1 5.4 %copy-start.4 = (bf16[3,128,320]{2,1,0:T(8,128)(2,1)S(1)}, bf16[3,128,320]{2,1,0:T(8,128)(2,1)}, u32[]{:S(2)}) copy-start(bf16[3,128,320]{2,1,0:T(8,128)(2,1)} %copy.35) | copy-start | bytes 737284
  109.3 6.8 %copy-start.3 = (bf16[3,128,320]{2,1,0:T(8,128)(2,1)S(1)}, bf16[3,128,320]{2,1,0:T(8,128)(2,1)}, u32[]{:S(2)}) copy-start(bf16[3,128,320]{2,1,0:T(8,128)(2,1)} %copy.37) | copy-start | bytes 737284
  111.3 6.4 %copy-start.8 = (bf16[3,128,320]{2,1,0:T(8,128)(2,1)S(1)}, bf16[3,128,320]{2,1,0:T(8,128)(2,1)}, u32[]{:S(2)}) copy-start(bf16[3,128,320]{2,1,0:T(8,128)(2,1)} %copy.30) | copy-start | bytes 737284
  112.9 6.3 %copy-start.9 = (bf16[3,128,320]{2,1,0:T(8,128)(2,1)S(1)}, bf16[3,128,320]{2,1,0:T(8,128)(2,1)}, u32[]{:S(2)}) copy-start(bf16[3,128,320]{2,1,0:T(8,128)(2,1)} %copy.36) | copy-start | bytes 737284
  114.5 6.3 %copy-start.2 = (bf16[384,320]{1,0:T(8,128)(2,1)S(1)}, bf16[384,320]{1,0:T(8,128)(2,1)}, u32[]{:S(2)}) copy-start(bf16[384,320]{1,0:T(8,128)(2,1)} %bitcast_multiply_fusion.1) | copy-start | bytes 737284
  116.1 6.2 %copy-start.1 = (bf16[3,128,320]{2,1,0:T(8,128)(2,1)S(1)}, bf16[3,128,320]{2,1,0:T(8,128)(2,1)}, u32[]{:S(2)}) copy-start(bf16[3,128,320]{2,1,0:T(8,128)(2,1)} %copy.29) | copy-start | bytes 737284
  116.1 6.2 %copy-start.30 = (f32[384]{0:T(512)S(1)}, f32[384]{0:T(512)}, u32[]{:S(2)}) copy-start(f32[384]{0:T(512)} %get-tuple-element.34) | copy-start | bytes 4612
  124.4 45.5 %copy-start.20 = (f32[360,320]{0,1:T(8,128)S(1)}, f32[360,320]{0,1:T(8,128)}, u32[]{:S(2)}) copy-start(f32[360,320]{0,1:T(8,128)} %param.15) | copy-start | bytes 1382404
  124.4 45.4 %copy-start.21 = (f32[360,320]{0,1:T(8,128)S(1)}, f32[360,320]{0,1:T(8,128)}, u32[]{:S(2)}) copy-start(f32[360,320]{0,1:T(8,128)} %param.14) | copy-start | bytes 1382404
  124.6 4.1 %collective-permute-start.15 = (f32[32]{0:T(128)S(1)}, f32[32]{0:T(128)S(1)}, u32[]{:S(2)}, u32[]{:S(2)}) collective-permute-start(f32[32]{0:T(128)S(1)} %reduce_sum.72), channel_id=1, source_target_pairs={{0,8},{8,0},{16,24},{24,16},{1,9},{9,1},{17,25},{25,17},{2,10},{10... | collective-permute-start | bytes 392 | tf_op jit(solution)/shard_map/ppermute | solution.py:33
  127.4 3.6 %collective-permute-start.17 = (f32[32]{0:T(128)S(1)}, f32[32]{0:T(128)S(1)}, u32[]{:S(2)}, u32[]{:S(2)}) collective-permute-start(f32[32]{0:T(128)S(1)} %reduce_sum.75), channel_id=1, source_target_pairs={{0,8},{8,0},{16,24},{24,16},{1,9},{9,1},{17,25},{25,17},{2,10},{10... | collective-permute-start | bytes 392 | tf_op jit(solution)/shard_map/ppermute | solution.py:33
  128.7 4.4 %collective-permute-start.16 = (f32[32]{0:T(128)S(1)}, f32[32]{0:T(128)S(1)}, u32[]{:S(2)}, u32[]{:S(2)}) collective-permute-start(f32[32]{0:T(128)S(1)} %add.214), channel_id=1, source_target_pairs={{0,16},{8,24},{16,0},{24,8},{1,17},{9,25},{17,1},{25,9},{2,18},{10... | collective-permute-start | bytes 392 | tf_op jit(solution)/shard_map/ppermute | solution.py:33
  131.0 4.4 %collective-permute-start.18 = (f32[32]{0:T(128)S(1)}, f32[32]{0:T(128)S(1)}, u32[]{:S(2)}, u32[]{:S(2)}) collective-permute-start(f32[32]{0:T(128)S(1)} %add.216), channel_id=1, source_target_pairs={{0,16},{8,24},{16,0},{24,8},{1,17},{9,25},{17,1},{25,9},{2,18},{10... | collective-permute-start | bytes 392 | tf_op jit(solution)/shard_map/ppermute | solution.py:33
Sparse Core Ops, SparseCore 0:
  84.9 40.9 reduce-scatter.1
  136.0 33.7 all-reduce.3
